TPU v7x, 256 devices: a whole 4x4x8 slice. The times are simulated.
256 devices in a mesh: gx: 16 (over y, z_lo), gy: 16 (over x, z_hi, core).
Axes of the slice: x: 4, y: 4, z: 8 (z_hi: 2, z_lo: 4; z = z_hi * 4 + z_lo), core: 2. Of those that a mesh axis runs over, the one named last changes fastest.
Arguments:
- load_vectors: float32 [16, 16, 8, 8, 192], P('gx', 'gy'), may hold values from -45 to 45
- bond_stiffness: bfloat16 [16, 16, 8, 13, 36864], P('gx', 'gy'), may hold values from 0 to 0.0016937256
- intact_words: int32 [16, 16, 8, 13, 64, 4], P('gx', 'gy'), may hold values from 0 to 65535
- block_cols: int32 [16, 16, 8, 13], P('gx', 'gy'), may hold values from 0 to 89, as said below
- self_stiffness: bfloat16 [16, 16, 8, 36864], P('gx', 'gy'), may hold values from -0.01 to 3.01, as said below
- block_inverse: float32 [16, 16, 8, 36864], P('gx', 'gy'), may hold values from -0.01 to 0.61, as said below
- coarse_basis: float32 [16, 16, 16, 8, 192], P('gx', 'gy'), may hold values from -0.3 to 0.3
- coarse_factor: float32 [4096, 4096], P(('gx', 'gy')), may hold values from -0.375 to 0.375
Outputs:
- displacement: float32 [16, 16, 8, 8, 192], P('gx', 'gy')
- residual: float32 [16, 16, 8, 8, 192], P('gx', 'gy')
Inputs may be any that keep to these rules, and one draw needn't show every extreme that they name: `block_cols`: the 13 codes of a block name different blocks among the 26 around it (never the block itself), each |a - 1|, |c - 1|, |w - 1 - z| at most 1. `self_stiffness`: each block, read as a matrix, is symmetric. `block_inverse`: each block, read as a matrix, is symmetric.
All inputs are finite; a program needn't handle non-finite values.
Results may differ from a plain program's by a relative error of at most 0.0055.
Values may be sent and summed in bfloat16 or wider, within the bound.
No kernel may reach another device: no remote copies, remote signals or barrier semaphores. Data moves between devices by JAX's collectives and lax.ppermute only.
A program may use at most 128 MiB of HBM per device.

v0:
```python
import jax
import jax.numpy as jnp
from jax import lax
from jax.sharding import PartitionSpec as P

COMP = 3
PB = 64
DOF = 192
NS = 13
BZ = 8
NLOAD = 8
ITERS = 2
highest = lax.Precision.HIGHEST


def padded_2(x, sides, width):
    for axis, dim in sides:
        size, length = (lax.axis_size(axis), x.shape[dim])
        up = [(i, (i + 1) % size) for i in range(size - 1)]
        down = [(j, i) for i, j in up]
        last = lax.slice_in_dim(x, length - width, length, axis=dim)
        initial = lax.slice_in_dim(x, 0, width, axis=dim)
        before = lax.ppermute(last, axis, up)
        after = lax.ppermute(initial, axis, down)
        x = jnp.concatenate([before, x, after], axis=dim)
    return x


def unpack_bits(packed):
    shifts = jnp.arange(16, dtype=jnp.int32)
    bitset = jnp.right_shift(packed[..., None], shifts) & 1
    return bitset.reshape(packed.shape[:-1] + (packed.shape[-1] * 16,))


def masked_blocks(stiffness, packed):
    intact = unpack_bits(packed).astype(stiffness.dtype)
    leading = stiffness.shape[:-1]
    shaped = stiffness.reshape(leading + (COMP, PB, COMP, PB))
    masked = shaped * intact[..., None, :, None, :]
    return masked.reshape(leading + (DOF, DOF))


def per_device(
    load_vectors,
    bond_stiffness,
    intact_words,
    block_cols,
    self_stiffness,
    block_inverse,
    coarse_basis,
    coarse_factor,
):
    weights = masked_blocks(bond_stiffness[0, 0], intact_words[0, 0])
    row_total = jnp.sum(weights, axis=(1, 3), dtype=jnp.float32)
    column_total = jnp.sum(weights, axis=2, dtype=jnp.float32)
    col_codes = block_cols[0, 0]
    depth_span = BZ + 2
    ghost_count = 9 * depth_span
    selector = (
        jnp.arange(ghost_count, dtype=jnp.int32)[:, None] == col_codes.reshape(-1)[None, :]
    ).astype(jnp.bfloat16)
    self_block = self_stiffness[0, 0].reshape(BZ, DOF, DOF)
    inverse = block_inverse[0, 0].reshape(BZ, DOF, DOF)
    coarse_vecs = coarse_basis[0, 0]

    def smooth_local(field):
        return jnp.einsum("bij,blj->bli", inverse, field, precision=highest)

    def restrict(field):
        restricted = jnp.einsum("kbi,bli->lk", coarse_vecs, field, precision=highest)
        return jnp.dot(restricted, coarse_factor, precision=highest)

    def prolong(summed):
        spread = jnp.einsum("lc,kc->lk", summed, coarse_factor, precision=highest)
        return jnp.einsum("kbi,lk->bli", coarse_vecs, spread, precision=highest)

    def precondition(residual):
        own_part = smooth_local(residual)
        coarse_term = restrict(residual)
        summed = lax.psum(coarse_term, ("gx", "gy"))
        smoothed = own_part + prolong(summed)
        energy = lax.psum(jnp.sum(residual * smoothed, axis=(0, 2)), ("gx", "gy"))
        return (smoothed, energy)

    residual = load_vectors[0, 0]
    solution = jnp.zeros_like(residual)
    smoothed, energy = precondition(residual)
    direction = smoothed
    for iteration in range(ITERS):
        rounded = direction.astype(jnp.bfloat16)
        ghosts = padded_2(rounded[None, None], (("gx", 0), ("gy", 1)), 1)
        padded = jnp.pad(ghosts, ((0, 0), (0, 0), (1, 1), (0, 0), (0, 0))).reshape(
            ghost_count, NLOAD, DOF
        )
        gathered = jnp.take(padded, col_codes, axis=0)
        forward = row_total[:, None, :] * rounded - jnp.einsum(
            "bsij,bslj->bli", weights, gathered, preferred_element_type=jnp.float32
        )
        backward = column_total[:, :, None, :] * gathered - jnp.einsum(
            "bsij,bli->bslj", weights, rounded, preferred_element_type=jnp.float32
        )
        flat_terms = backward.reshape(BZ * NS, NLOAD * DOF)
        high_part = flat_terms.astype(jnp.bfloat16)
        low_part = (flat_terms - high_part.astype(jnp.float32)).astype(jnp.bfloat16)
        apply_spread = jnp.dot(selector, high_part, preferred_element_type=jnp.float32) + jnp.dot(
            selector, low_part, preferred_element_type=jnp.float32
        )
        partial_value = apply_spread.reshape(3, 3, depth_span, NLOAD, DOF)[:, :, 1 : depth_span - 1]
        beside_all = padded_2(partial_value.astype(jnp.bfloat16), (("gx", 0), ("gy", 1)), 1).astype(
            partial_value.dtype
        )
        folded = (
            beside_all[2, 2]
            + beside_all[0, 0]
            + beside_all[0, 2]
            + beside_all[0, 4]
            + beside_all[2, 0]
        )
        folded = folded + beside_all[2, 4] + beside_all[4, 0] + beside_all[4, 2] + beside_all[4, 4]
        diagonal = jnp.einsum(
            "bij,blj->bli", self_block, rounded, preferred_element_type=jnp.float32
        )
        operator_out = diagonal + forward + folded
        curve_sum = lax.psum(jnp.sum(direction * operator_out, axis=(0, 2)), ("gx", "gy"))
        step_scale = (energy / curve_sum)[None, :, None]
        solution = solution + step_scale * direction
        residual = residual - step_scale * operator_out
        if iteration + 1 < ITERS:
            smoothed, new_energy = precondition(residual)
            direction = smoothed + (new_energy / energy)[None, :, None] * direction
            energy = new_energy
    return (solution[None, None], residual[None, None])


def solution(mesh):
    in_specs = (
        P("gx", "gy", None, None, None),
        P("gx", "gy", None, None, None),
        P("gx", "gy", None, None, None, None),
        P("gx", "gy", None, None),
        P("gx", "gy", None, None),
        P("gx", "gy", None, None),
        P("gx", "gy", None, None, None),
        P(("gx", "gy"), None),
    )
    out_specs = (P("gx", "gy", None, None, None), P("gx", "gy", None, None, None))
    return jax.shard_map(
        per_device, mesh=mesh, in_specs=in_specs, out_specs=out_specs, check_vma=False
    )
```

profile of v0, /device:TPU:1, one launch (start us, length us, event | category | flops | bytes accessed | tf_op | source)
XLA Modules:
  0.0 896.7 jit_solution(10883457999654128121)
XLA Ops:
  11.5 2.9 fusion.63
  15.9 2.9 copy.45
  18.9 8.8 mul.97
  27.7 34.7 %mul.102 = bf16[8,13,192,192]{3,2,1,0:T(8,128)(2,1)} reshape(bf16[8,13,3,64,3,64]{5,4,3,2,1,0:T(4,128)(2,1)} %mul.97) | data formatting | bytes 15335424 | tf_op jit(solution)/shard_map/mul | solution.py:39
  62.3 16.6 %reshape_squeeze.11 = bf16[8,13,192,192]{3,2,0,1:T(8,128)(2,1)} reshape(bf16[1,1,8,13,36864]{4,2,3,1,0:T(8,128)(2,1)} %param.11) | data formatting | bytes 15335424 | tf_op jit(solution)/shard_map/reshape;squeeze | solution.py:38
  79.0 14.1 %convert_reduce_fusion = (f32[8,13,192]{2,0,1:T(8,128)S(1)}, bf16[8,13,192,192]{3,2,0,1:T(8,128)(2,1)}) fusion(bf16[8,13,192,192]{3,2,0,1:T(8,128)(2,1)} %reshape_squeeze.11, bf16[8,13,192,192]{3,2,1,0:T(8,128)(2,1)} %mul.102), kind=kLoop, calls=%fused_computation.2 | loop fusion | flops 11481600 | bytes 23083008 | tf_op jit(solution)/shard_map/reduce_sum | solution.py:55
  93.1 168.8 %all-reduce.6.cloned.1.call-done = f32[8,4096]{1,0:T(8,128)} async-done(((f32[8,4096]{1,0:T(8,128)}), f32[8,4096]{1,0:T(8,128)}) %all-reduce.6.cloned.1.call-update) | async-done | bytes 131088 | tf_op jit(solution)/shard_map/psum | solution.py:80
  264.1 3.8 collective-permute-start
  269.2 19.7 %reshape.113 = bf16[1,1,8,13,36864]{4,3,2,1,0:T(8,128)(2,1)} reshape(bf16[8,13,3,64,3,64]{5,4,3,2,1,0:T(4,128)(2,1)} %mul.97) | data formatting | bytes 15335424 | tf_op jit(solution)/shard_map/mul | solution.py:39
  289.1 3.5 collective-permute-start.2
  294.6 8.0 collective-permute-done.3
  304.0 5.4 fusion.21
  311.2 4.8 collective-permute-start.4
  317.5 11.9 %convert_reduce_fusion.1 = f32[8,36864]{1,0:T(8,128)} fusion(bf16[1,1,8,13,36864]{4,2,3,1,0:T(8,128)(2,1)} %param.11, bf16[1,1,8,13,36864]{4,3,2,1,0:T(8,128)(2,1)} %reshape.113), kind=kLoop, calls=%fused_computation.3 | loop fusion | flops 11206656 | bytes 16515072 | tf_op jit(solution)/shard_map/reduce_sum | solution.py:54
  331.4 2.9 reshape_squeeze.10
  339.3 2.2 collective-permute-start.7
  341.5 6.7 fusion.35
  348.2 3.0 collective-permute-done.7
  352.5 81.6 %all-reduce.2 = (f32[8]{0:T(128)S(1)}, f32[8]{0:T(128)S(1)}) all-reduce(f32[8]{0:T(128)S(1)} %get-tuple-element.4, f32[8]{0:T(128)S(1)} %get-tuple-element.3), channel_id=1, replica_groups=mesh['gx'=16,'gy'=16] {'gx','gy'}, use_global_device_ids=true, to_apply=%region_2.0 | all-reduce | flops 16 | bytes 128 | tf_op jit(solution)/shard_map/psum | solution.py:82
  436.7 240.2 %all-reduce.8.cloned.1.call-done = f32[8,4096]{1,0:T(8,128)} async-done(((f32[8,4096]{1,0:T(8,128)}), f32[8,4096]{1,0:T(8,128)}) %all-reduce.8.cloned.1.call-update) | async-done | bytes 131088 | tf_op jit(solution)/shard_map/psum | solution.py:80
  678.6 76.3 %psum.46 = f32[8]{0:T(128)S(1)} all-reduce(f32[8]{0:T(128)S(1)} %get-tuple-element.24), channel_id=1, replica_groups=mesh['gx'=16,'gy'=16] {'gx','gy'}, use_global_device_ids=true, to_apply=%region_10.12 | all-reduce | flops 8 | bytes 64 | tf_op jit(solution)/shard_map/psum | solution.py:82
  755.0 2.4 collective-permute-start.8
  758.7 3.7 collective-permute-done.9
  762.4 6.5 collective-permute-start.10
  770.8 8.0 collective-permute-done.11
  779.5 4.8 fusion.18
  785.4 2.4 collective-permute-start.12
  789.3 3.7 collective-permute-done.13
  793.2 4.2 collective-permute-start.14
  799.3 5.5 fusion.32
  804.8 4.5 collective-permute-done.15
  809.7 79.3 %psum.47 = f32[8]{0:T(128)S(1)} all-reduce(f32[8]{0:T(128)S(1)} %get-tuple-element.7), channel_id=1, replica_groups=mesh['gx'=16,'gy'=16] {'gx','gy'}, use_global_device_ids=true, to_apply=%region_12.14 | all-reduce | flops 8 | bytes 64 | tf_op jit(solution)/shard_map/psum | solution.py:124
  (97 shorter events, 38.6 us)
Async XLA Ops:
  7.2 1.3 copy-start
  7.2 254.7 %all-reduce.6.cloned.1.call-start = ((), (), s32[]{:S(2)}) async-start(), calls=%async_computation | async-start | bytes 262144 | tf_op jit(solution)/shard_map/psum | solution.py:80
  9.4 667.5 %all-reduce.8.cloned.1.call-start = ((), (), s32[]{:S(2)}) async-start(), calls=%async_computation.1 | async-start | bytes 262144 | tf_op jit(solution)/shard_map/psum | solution.py:80
  79.0 14.1 %copy-start.11 = (s32[1,1,8,13]{3,2,1,0:T(8,128)S(1)}, s32[1,1,8,13]{3,2,1,0:T(8,128)}, u32[]{:S(2)}) copy-start(s32[1,1,8,13]{3,2,1,0:T(8,128)} %param.13) | copy-start | bytes 1252
  79.0 184.2 %copy-start.2 = (f32[1,1,16,8,192]{4,3,2,1,0:T(8,128)S(1)}, f32[1,1,16,8,192]{4,3,2,1,0:T(8,128)}, u32[]{:S(2)}) copy-start(f32[1,1,16,8,192]{4,3,2,1,0:T(8,128)} %param.16) | copy-start | bytes 294916
  79.0 184.2 %copy-start.10 = (f32[8,8,192]{2,1,0:T(8,128)S(1)}, f32[8,8,192]{2,1,0:T(8,128)}, u32[]{:S(2)}) copy-start(f32[8,8,192]{2,1,0:T(8,128)} %fusion.63) | copy-start | bytes 147460
  264.1 39.9 %copy-start.8 = (bf16[8,8,192]{2,1,0:T(8,128)(2,1)}, bf16[8,8,192]{2,1,0:T(8,128)(2,1)S(1)}, u32[]{:S(2)}) copy-start(bf16[8,8,192]{2,1,0:T(8,128)(2,1)S(1)} %get-tuple-element.22) | copy-start | bytes 73732
  264.1 25.0 %collective-permute-start = (bf16[1,1,8,8,192]{4,3,2,1,0:T(8,128)(2,1)S(1)}, bf16[1,1,8,8,192]{4,3,2,1,0:T(8,128)(2,1)S(1)}, u32[]{:S(2)}, u32[]{:S(2)}) collective-permute-start(bf16[1,1,8,8,192]{4,3,2,1,0:T(8,128)(2,1)S(1)} %bitcast.127), channel_id=1, source_target_pairs={{0,16},{16,32},{32,48},{48,64},{64,80},{80,96},{96,112},{112,128},... | collective-permute-start | bytes 73736 | tf_op jit(solution)/shard_map/ppermute | solution.py:23
  267.9 21.2 %collective-permute-start.1 = (bf16[1,1,8,8,192]{4,3,2,1,0:T(8,128)(2,1)S(1)}, bf16[1,1,8,8,192]{4,3,2,1,0:T(8,128)(2,1)S(1)}, u32[]{:S(2)}, u32[]{:S(2)}) collective-permute-start(bf16[1,1,8,8,192]{4,3,2,1,0:T(8,128)(2,1)S(1)} %bitcast.128), channel_id=1, source_target_pairs={{16,0},{32,16},{48,32},{64,48},{80,64},{96,80},{112,96},{128,112},... | collective-permute-start | bytes 73736 | tf_op jit(solution)/shard_map/ppermute | solution.py:24
  289.0 15.0 %copy-start.4 = (f32[8,13,192]{2,1,0:T(8,128)}, f32[8,13,192]{2,1,0:T(8,128)S(1)}, u32[]{:S(2)}) copy-start(f32[8,13,192]{2,1,0:T(8,128)S(1)} %copy.49) | copy-start | bytes 239620
  289.1 5.5 collective-permute-start.2
  292.6 9.9 %collective-permute-start.3 = (bf16[3,1,8,8,192]{4,3,2,1,0:T(8,128)(2,1)S(1)}, bf16[3,1,8,8,192]{4,3,2,1,0:T(8,128)(2,1)S(1)}, u32[]{:S(2)}, u32[]{:S(2)}) collective-permute-start(bf16[3,1,8,8,192]{4,3,2,1,0:T(8,128)(2,1)S(1)} %pad_maximum_fusion.6), channel_id=1, source_target_pairs={{1,0},{2,1},{3,2},{4,3},{5,4},{6,5},{7,6},{8,7},{9,8},{10,9},{11,1... | collective-permute-start | bytes 221192 | tf_op jit(solution)/shard_map/ppermute | solution.py:24
  310.5 7.0 copy-start.3
  311.2 25.0 %collective-permute-start.4 = (bf16[1,3,8,8,192]{4,3,2,1,0:T(8,128)(2,1)}, bf16[1,3,8,8,192]{4,3,2,1,0:T(8,128)(2,1)}, u32[]{:S(2)}, u32[]{:S(2)}) collective-permute-start(bf16[1,3,8,8,192]{4,3,2,1,0:T(8,128)(2,1)} %get-tuple-element.18), channel_id=1, source_target_pairs={{0,16},{16,32},{32,48},{48,64},{64,80},{80,96},{96,112},{112,128},... | collective-permute-start | bytes 221192 | tf_op jit(solution)/shard_map/ppermute | solution.py:23
  316.0 20.3 %collective-permute-start.5 = (bf16[1,3,8,8,192]{4,3,2,1,0:T(8,128)(2,1)}, bf16[1,3,8,8,192]{4,3,2,1,0:T(8,128)(2,1)}, u32[]{:S(2)}, u32[]{:S(2)}) collective-permute-start(bf16[1,3,8,8,192]{4,3,2,1,0:T(8,128)(2,1)} %get-tuple-element.19), channel_id=1, source_target_pairs={{16,0},{32,16},{48,32},{64,48},{80,64},{96,80},{112,96},{128,112},... | collective-permute-start | bytes 221192 | tf_op jit(solution)/shard_map/ppermute | solution.py:24
  335.2 16.0 %copy-start.1 = (bf16[8,192,192]{2,1,0:T(8,128)(2,1)S(1)}, bf16[8,192,192]{2,1,0:T(8,128)(2,1)}, u32[]{:S(2)}) copy-start(bf16[8,192,192]{2,1,0:T(8,128)(2,1)} %reshape_squeeze.10) | copy-start | bytes 1769476
  335.2 16.0 %copy-start.6 = (f32[8,8,192]{2,1,0:T(8,128)S(1)}, f32[8,8,192]{2,1,0:T(8,128)}, u32[]{:S(2)}) copy-start(f32[8,8,192]{2,1,0:T(8,128)} %get-tuple-element.23) | copy-start | bytes 147460
  335.2 16.0 %copy-start.7 = (f32[1,1,8,8,192]{4,3,2,1,0:T(8,128)S(1)}, f32[1,1,8,8,192]{4,3,2,1,0:T(8,128)}, u32[]{:S(2)}) copy-start(f32[1,1,8,8,192]{4,3,2,1,0:T(8,128)} %param.10) | copy-start | bytes 147460
  335.2 16.0 %copy-start.9 = (bf16[8,8,192]{2,1,0:T(8,128)(2,1)S(1)}, bf16[8,8,192]{2,1,0:T(8,128)(2,1)}, u32[]{:S(2)}) copy-start(bf16[8,8,192]{2,1,0:T(8,128)(2,1)} %copy-done.8) | copy-start | bytes 73732
  335.2 444.3 %copy-start.5 = (f32[8,13,192]{2,1,0:T(8,128)S(1)}, f32[8,13,192]{2,1,0:T(8,128)}, u32[]{:S(2)}) copy-start(f32[8,13,192]{2,1,0:T(8,128)} %copy-done.4) | copy-start | bytes 239620
  337.2 11.0 %collective-permute-start.6 = (bf16[5,1,8,8,192]{4,3,2,1,0:T(8,128)(2,1)S(1)}, bf16[5,1,8,8,192]{4,3,2,1,0:T(8,128)(2,1)S(1)}, u32[]{:S(2)}, u32[]{:S(2)}) collective-permute-start(bf16[5,1,8,8,192]{4,3,2,1,0:T(8,128)(2,1)S(1)} %get-tuple-element.14), channel_id=1, source_target_pairs={{0,1},{1,2},{2,3},{3,4},{4,5},{5,6},{6,7},{7,8},{8,9},{9,10},{10,1... | collective-permute-start | bytes 368648 | tf_op jit(solution)/shard_map/ppermute | solution.py:23
  339.3 11.9 %collective-permute-start.7 = (bf16[5,1,8,8,192]{4,3,2,1,0:T(8,128)(2,1)S(1)}, bf16[5,1,8,8,192]{4,3,2,1,0:T(8,128)(2,1)S(1)}, u32[]{:S(2)}, u32[]{:S(2)}) collective-permute-start(bf16[5,1,8,8,192]{4,3,2,1,0:T(8,128)(2,1)S(1)} %get-tuple-element.15), channel_id=1, source_target_pairs={{1,0},{2,1},{3,2},{4,3},{5,4},{6,5},{7,6},{8,7},{9,8},{10,9},{11,1... | collective-permute-start | bytes 368648 | tf_op jit(solution)/shard_map/ppermute | solution.py:24
  678.2 121.1 %copy-start.12 = (f32[8,192]{1,0:T(8,128)S(1)}, f32[8,192]{1,0:T(8,128)}, u32[]{:S(2)}) copy-start(f32[8,192]{1,0:T(8,128)} %reduce_sum.64) | copy-start | bytes 18436
  755.0 3.7 collective-permute-start.8
  757.4 5.0 collective-permute-start.9
  762.4 8.4 collective-permute-start.10
  768.9 9.9 %collective-permute-start.11 = (bf16[3,1,8,8,192]{4,3,2,1,0:T(8,128)(2,1)S(1)}, bf16[3,1,8,8,192]{4,3,2,1,0:T(8,128)(2,1)S(1)}, u32[]{:S(2)}, u32[]{:S(2)}) collective-permute-start(bf16[3,1,8,8,192]{4,3,2,1,0:T(8,128)(2,1)S(1)} %pad_maximum_fusion.7), channel_id=1, source_target_pairs={{1,0},{2,1},{3,2},{4,3},{5,4},{6,5},{7,6},{8,7},{9,8},{10,9},{11,1... | collective-permute-start | bytes 221192 | tf_op jit(solution)/shard_map/ppermute | solution.py:24
  785.4 4.0 collective-permute-start.12
  787.7 5.4 collective-permute-start.13
  793.2 11.6 %collective-permute-start.14 = (bf16[5,1,8,8,192]{4,3,2,1,0:T(8,128)(2,1)S(1)}, bf16[5,1,8,8,192]{4,3,2,1,0:T(8,128)(2,1)S(1)}, u32[]{:S(2)}, u32[]{:S(2)}) collective-permute-start(bf16[5,1,8,8,192]{4,3,2,1,0:T(8,128)(2,1)S(1)} %get-tuple-element.12), channel_id=1, source_target_pairs={{0,1},{1,2},{2,3},{3,4},{4,5},{5,6},{6,7},{7,8},{8,9},{9,10},{10,1... | collective-permute-start | bytes 368648 | tf_op jit(solution)/shard_map/ppermute | solution.py:23
  797.4 11.9 %collective-permute-start.15 = (bf16[5,1,8,8,192]{4,3,2,1,0:T(8,128)(2,1)S(1)}, bf16[5,1,8,8,192]{4,3,2,1,0:T(8,128)(2,1)S(1)}, u32[]{:S(2)}, u32[]{:S(2)}) collective-permute-start(bf16[5,1,8,8,192]{4,3,2,1,0:T(8,128)(2,1)S(1)} %get-tuple-element.13), channel_id=1, source_target_pairs={{1,0},{2,1},{3,2},{4,3},{5,4},{6,5},{7,6},{8,7},{9,8},{10,9},{11,1... | collective-permute-start | bytes 368648 | tf_op jit(solution)/shard_map/ppermute | solution.py:24
Sparse Core Ops, SparseCore 0:
  13.5 248.3 all-reduce.5
  435.5 241.3 all-reduce.7
where the time goes:
time: 899 us; the launch traced here: 897 us
  waiting for transfers between devices  440 us (49%)
  blocking collectives  237 us (26%)
  local copies, waits for them, and re-layouts  94.9 us (11%)
  starting transfers between devices  43 us (5%)
  matrix products  36.3 us (4%)
  other arithmetic  30.5 us (3%)
  between operations  14.5 us (2%)
    psum x2, waiting for transfers between devices, precondition(): summed = lax.psum(coarse_term, ('gx', 'gy'))  409 us
    psum x2, blocking collectives, precondition(): energy = lax.psum(jnp.sum(residual * smoothed, axis=(0, 2)), ('gx', 'gy'))  158 us
    psum x1, blocking collectives, per_device(): lax.psum(jnp.sum(direction * operator_out, axis=(0, 2)), ('gx', 'gy'))  79.3 us
    mul x3, local copies, waits for them, and re-layouts, masked_blocks(): masked = shaped * intact[..., None, :, None, :]  63.1 us
    ppermute x8, waiting for transfers between devices, padded_2(): after = lax.ppermute(initial, axis, down)  30.9 us
    ppermute x8, starting transfers between devices, padded_2(): before = lax.ppermute(last, axis, up)  29.6 us
  transfers between devices with their start and end apart: 18, of which 9 were waited for; matrix products, arithmetic and copies ran while one was open for 15% of the time, Pallas kernels for 0%

commit v1 on v0

--- a/solution.py
+++ b/solution.py
@@ -1,7 +1,9 @@
+import functools
 import jax
 import jax.numpy as jnp
 from jax import lax
 from jax.sharding import PartitionSpec as P
+from jax.lax import all_gather
 
 COMP = 3
 PB = 64
@@ -11,6 +13,14 @@
 NLOAD = 8
 ITERS = 2
 highest = lax.Precision.HIGHEST
+
+
+def _put_column(local_array, net_axis):
+    moved = all_gather(local_array, net_axis)
+    return jnp.sum(moved, axis=0)
+
+
+remake_meshes_up = functools.partial(_put_column, net_axis=("gx", "gy"))
 
 
 def padded_2(x, sides, width):
@@ -77,7 +87,7 @@
     def precondition(residual):
         own_part = smooth_local(residual)
         coarse_term = restrict(residual)
-        summed = lax.psum(coarse_term, ("gx", "gy"))
+        summed = remake_meshes_up(coarse_term)
         smoothed = own_part + prolong(summed)
         energy = lax.psum(jnp.sum(residual * smoothed, axis=(0, 2)), ("gx", "gy"))
         return (smoothed, energy)

time: 899 us -> 1310 us (1.46)
  waiting for transfers between devices: 440 us -> 809 us
  other arithmetic: 30.5 us -> 54.6 us
  starting transfers between devices: 43 us -> 64.3 us
    all_gather x0 -> x2, waiting for transfers between devices: none -> 803 us  [_put_column(): moved = all_gather(local_array, net_axis)]
    psum x2 -> x0, waiting for transfers between devices: 409 us -> none  [precondition(): summed = lax.psum(coarse_term, ('gx', 'gy'))]
    ppermute x8, waiting for transfers between devices: 30.9 us -> 0.86 us  [padded_2(): after = lax.ppermute(initial, axis, down)]
    reduce_sum x0 -> x2, other arithmetic: none -> 24.1 us  [_put_column(): return jnp.sum(moved, axis=0)]
    ppermute x8, starting transfers between devices: 29.6 us -> 45.9 us  [padded_2(): before = lax.ppermute(last, axis, up)]
  transfers between devices with their start and end apart: 18 -> 18, of which waited for: 9 -> 8; matrix products, arithmetic and copies ran while one was open for 15% -> 10% of each run, Pallas kernels for 0% -> 0%
where the time goes in v1:
time: 1310 us
  waiting for transfers between devices  809 us (62%)
  blocking collectives  238 us (18%)
  local copies, waits for them, and re-layouts  95.2 us (7%)
  starting transfers between devices  64.3 us (5%)
  other arithmetic  54.6 us (4%)
  matrix products  33 us (3%)
  between operations  14.5 us (1%)
    all_gather x2, waiting for transfers between devices, _put_column(): moved = all_gather(local_array, net_axis)  803 us
    psum x2, blocking collectives, precondition(): energy = lax.psum(jnp.sum(residual * smoothed, axis=(0, 2)), ('gx', 'gy'))  155 us
    psum x1, blocking collectives, per_device(): lax.psum(jnp.sum(direction * operator_out, axis=(0, 2)), ('gx', 'gy'))  83 us
    mul x3, local copies, waits for them, and re-layouts, masked_blocks(): masked = shaped * intact[..., None, :, None, :]  63.4 us
    ppermute x8, starting transfers between devices, padded_2(): before = lax.ppermute(last, axis, up)  45.9 us
  transfers between devices with their start and end apart: 18, of which 8 were waited for; matrix products, arithmetic and copies ran while one was open for 10% of the time, Pallas kernels for 0%

profile of v1, /device:TPU:1, one launch (start us, length us, event | category | flops | bytes accessed | tf_op | source)
XLA Modules:
  0.0 1308.6 jit_solution(5038043465383825100)
XLA Ops:
  9.5 2.0 reshape_squeeze.9
  11.5 16.6 %reshape_squeeze.11 = bf16[8,13,192,192]{3,2,0,1:T(8,128)(2,1)} reshape(bf16[1,1,8,13,36864]{4,2,3,1,0:T(8,128)(2,1)} %param.11) | data formatting | bytes 15335424 | tf_op jit(solution)/shard_map/reshape;squeeze | solution.py:48
  29.7 3.0 copy.45
  32.7 8.9 mul.97
  41.6 34.8 %mul.102 = bf16[8,13,192,192]{3,2,1,0:T(8,128)(2,1)} reshape(bf16[8,13,3,64,3,64]{5,4,3,2,1,0:T(4,128)(2,1)} %mul.97) | data formatting | bytes 15335424 | tf_op jit(solution)/shard_map/mul | solution.py:49
  77.8 14.1 %convert_reduce_fusion = (f32[8,13,192]{2,0,1:T(8,128)S(1)}, bf16[8,13,192,192]{3,2,0,1:T(8,128)(2,1)}) fusion(bf16[8,13,192,192]{3,2,0,1:T(8,128)(2,1)} %reshape_squeeze.11, bf16[8,13,192,192]{3,2,1,0:T(8,128)(2,1)} %mul.102), kind=kLoop, calls=%fused_computation.4 | loop fusion | flops 11481600 | bytes 23083008 | tf_op jit(solution)/shard_map/reduce_sum | solution.py:65
  91.9 365.9 %all-gather.5.cloned.1.call-done = f32[2048,4096]{1,0:T(8,128)} async-done(((f32[8,4096]{1,0:T(8,128)}), f32[2048,4096]{1,0:T(8,128)}) %all-gather.5.cloned.1.call-update) | async-done | bytes 33554448 | tf_op jit(solution)/shard_map/all_gather | solution.py:19
  457.8 12.1 bitcast_reduce_fusion.1
  472.4 4.0 collective-permute-start
  476.5 19.7 %reshape.115 = bf16[1,1,8,13,36864]{4,3,2,1,0:T(8,128)(2,1)} reshape(bf16[8,13,3,64,3,64]{5,4,3,2,1,0:T(4,128)(2,1)} %mul.97) | data formatting | bytes 15335424 | tf_op jit(solution)/shard_map/mul | solution.py:49
  496.4 5.6 collective-permute-start.3
  502.0 5.3 collective-permute-start.2
  510.3 5.4 fusion.21
  518.8 4.6 collective-permute-start.4
  523.4 11.9 convert_reduce_fusion.1
  535.3 2.0 reduce_sum.82
  537.3 2.9 reshape_squeeze.10
  545.0 8.8 collective-permute-start.6
  553.8 6.7 fusion.35
  561.8 80.1 %all-reduce.2 = (f32[8]{0:T(128)S(1)}, f32[8]{0:T(128)S(1)}) all-reduce(f32[8]{0:T(128)S(1)} %get-tuple-element.4, f32[8]{0:T(128)S(1)} %get-tuple-element.3), channel_id=1, replica_groups=mesh['gx'=16,'gy'=16] {'gx','gy'}, use_global_device_ids=true, to_apply=%region_2.0 | all-reduce | flops 16 | bytes 128 | tf_op jit(solution)/shard_map/psum | solution.py:92
  644.6 437.4 %all-gather.7.cloned.1.call-done = f32[2048,4096]{1,0:T(8,128)} async-done(((f32[8,4096]{1,0:T(8,128)}), f32[2048,4096]{1,0:T(8,128)}) %all-gather.7.cloned.1.call-update) | async-done | bytes 33554448 | tf_op jit(solution)/shard_map/all_gather | solution.py:19
  1082.0 12.1 bitcast_reduce_fusion
  1094.8 74.6 %psum.30 = f32[8]{0:T(128)S(1)} all-reduce(f32[8]{0:T(128)S(1)} %get-tuple-element.24), channel_id=1, replica_groups=mesh['gx'=16,'gy'=16] {'gx','gy'}, use_global_device_ids=true, to_apply=%region_10.12 | all-reduce | flops 8 | bytes 64 | tf_op jit(solution)/shard_map/psum | solution.py:92
  1170.8 4.0 collective-permute-start.8
  1175.8 3.7 collective-permute-start.11
  1179.5 5.8 collective-permute-start.10
  1187.7 4.8 fusion.18
  1194.9 4.2 collective-permute-start.12
  1200.8 1.9 collective-permute-start.15
  1202.7 9.4 collective-permute-start.14
  1212.1 5.5 fusion.32
  1218.0 83.0 %psum.31 = f32[8]{0:T(128)S(1)} all-reduce(f32[8]{0:T(128)S(1)} %get-tuple-element.7), channel_id=1, replica_groups=mesh['gx'=16,'gy'=16] {'gx','gy'}, use_global_device_ids=true, to_apply=%region_12.14 | all-reduce | flops 8 | bytes 64 | tf_op jit(solution)/shard_map/psum | solution.py:134
  (99 shorter events, 33.7 us)
Async XLA Ops:
  7.2 1.3 copy-start
  7.2 450.6 %all-gather.5.cloned.1.call-start = ((), (), s32[]{:S(2)}) async-start(), calls=%async_computation | async-start | bytes 33685504 | tf_op jit(solution)/shard_map/all_gather | solution.py:19
  9.4 1072.5 %all-gather.7.cloned.1.call-start = ((), (), s32[]{:S(2)}) async-start(), calls=%async_computation.1 | async-start | bytes 33685504 | tf_op jit(solution)/shard_map/all_gather | solution.py:19
  41.6 34.8 %copy-start.11 = (s32[1,1,8,13]{3,2,1,0:T(8,128)S(1)}, s32[1,1,8,13]{3,2,1,0:T(8,128)}, u32[]{:S(2)}) copy-start(s32[1,1,8,13]{3,2,1,0:T(8,128)} %param.13) | copy-start | bytes 1252
  41.6 34.8 %copy-start.7 = (f32[1,1,8,8,192]{4,3,2,1,0:T(8,128)S(1)}, f32[1,1,8,8,192]{4,3,2,1,0:T(8,128)}, u32[]{:S(2)}) copy-start(f32[1,1,8,8,192]{4,3,2,1,0:T(8,128)} %param.10) | copy-start | bytes 147460
  91.9 378.3 %copy-start.2 = (f32[1,1,16,8,192]{4,3,2,1,0:T(8,128)S(1)}, f32[1,1,16,8,192]{4,3,2,1,0:T(8,128)}, u32[]{:S(2)}) copy-start(f32[1,1,16,8,192]{4,3,2,1,0:T(8,128)} %param.16) | copy-start | bytes 294916
  471.1 39.2 %copy-start.9 = (bf16[8,8,192]{2,1,0:T(8,128)(2,1)}, bf16[8,8,192]{2,1,0:T(8,128)(2,1)S(1)}, u32[]{:S(2)}) copy-start(bf16[8,8,192]{2,1,0:T(8,128)(2,1)S(1)} %get-tuple-element.22) | copy-start | bytes 73732
  471.1 25.2 %collective-permute-start.1 = (bf16[1,1,8,8,192]{4,3,2,1,0:T(8,128)(2,1)S(1)}, bf16[1,1,8,8,192]{4,3,2,1,0:T(8,128)(2,1)S(1)}, u32[]{:S(2)}, u32[]{:S(2)}) collective-permute-start(bf16[1,1,8,8,192]{4,3,2,1,0:T(8,128)(2,1)S(1)} %bitcast.131), channel_id=1, source_target_pairs={{16,0},{32,16},{48,32},{64,48},{80,64},{96,80},{112,96},{128,112},... | collective-permute-start | bytes 73736 | tf_op jit(solution)/shard_map/ppermute | solution.py:34
  472.4 23.9 %collective-permute-start = (bf16[1,1,8,8,192]{4,3,2,1,0:T(8,128)(2,1)S(1)}, bf16[1,1,8,8,192]{4,3,2,1,0:T(8,128)(2,1)S(1)}, u32[]{:S(2)}, u32[]{:S(2)}) collective-permute-start(bf16[1,1,8,8,192]{4,3,2,1,0:T(8,128)(2,1)S(1)} %bitcast.132), channel_id=1, source_target_pairs={{0,16},{16,32},{32,48},{48,64},{64,80},{80,96},{96,112},{112,128},... | collective-permute-start | bytes 73736 | tf_op jit(solution)/shard_map/ppermute | solution.py:33
  496.3 14.1 %copy-start.4 = (f32[8,13,192]{2,1,0:T(8,128)}, f32[8,13,192]{2,1,0:T(8,128)S(1)}, u32[]{:S(2)}) copy-start(f32[8,13,192]{2,1,0:T(8,128)S(1)} %copy.49) | copy-start | bytes 239620
  496.4 11.2 collective-permute-start.3
  502.0 6.9 collective-permute-start.2
  516.8 6.7 copy-start.3
  517.5 24.7 %collective-permute-start.5 = (bf16[1,3,8,8,192]{4,3,2,1,0:T(8,128)(2,1)}, bf16[1,3,8,8,192]{4,3,2,1,0:T(8,128)(2,1)}, u32[]{:S(2)}, u32[]{:S(2)}) collective-permute-start(bf16[1,3,8,8,192]{4,3,2,1,0:T(8,128)(2,1)} %get-tuple-element.19), channel_id=1, source_target_pairs={{16,0},{32,16},{48,32},{64,48},{80,64},{96,80},{112,96},{128,112},... | collective-permute-start | bytes 221192 | tf_op jit(solution)/shard_map/ppermute | solution.py:34
  518.8 23.4 %collective-permute-start.4 = (bf16[1,3,8,8,192]{4,3,2,1,0:T(8,128)(2,1)}, bf16[1,3,8,8,192]{4,3,2,1,0:T(8,128)(2,1)}, u32[]{:S(2)}, u32[]{:S(2)}) collective-permute-start(bf16[1,3,8,8,192]{4,3,2,1,0:T(8,128)(2,1)} %get-tuple-element.18), channel_id=1, source_target_pairs={{0,16},{16,32},{32,48},{48,64},{64,80},{80,96},{96,112},{112,128},... | collective-permute-start | bytes 221192 | tf_op jit(solution)/shard_map/ppermute | solution.py:33
  541.1 19.4 %copy-start.1 = (bf16[8,192,192]{2,1,0:T(8,128)(2,1)S(1)}, bf16[8,192,192]{2,1,0:T(8,128)(2,1)}, u32[]{:S(2)}) copy-start(bf16[8,192,192]{2,1,0:T(8,128)(2,1)} %reshape_squeeze.10) | copy-start | bytes 1769476
  541.1 19.4 %copy-start.6 = (f32[8,8,192]{2,1,0:T(8,128)S(1)}, f32[8,8,192]{2,1,0:T(8,128)}, u32[]{:S(2)}) copy-start(f32[8,8,192]{2,1,0:T(8,128)} %get-tuple-element.23) | copy-start | bytes 147460
  541.1 19.4 %copy-start.8 = (f32[1,1,8,8,192]{4,3,2,1,0:T(8,128)S(1)}, f32[1,1,8,8,192]{4,3,2,1,0:T(8,128)}, u32[]{:S(2)}) copy-start(f32[1,1,8,8,192]{4,3,2,1,0:T(8,128)} %param.10) | copy-start | bytes 147460
  541.1 19.4 %copy-start.10 = (bf16[8,8,192]{2,1,0:T(8,128)(2,1)S(1)}, bf16[8,8,192]{2,1,0:T(8,128)(2,1)}, u32[]{:S(2)}) copy-start(bf16[8,8,192]{2,1,0:T(8,128)(2,1)} %copy-done.9) | copy-start | bytes 73732
  543.1 17.4 %collective-permute-start.7 = (bf16[5,1,8,8,192]{4,3,2,1,0:T(8,128)(2,1)S(1)}, bf16[5,1,8,8,192]{4,3,2,1,0:T(8,128)(2,1)S(1)}, u32[]{:S(2)}, u32[]{:S(2)}) collective-permute-start(bf16[5,1,8,8,192]{4,3,2,1,0:T(8,128)(2,1)S(1)} %get-tuple-element.15), channel_id=1, source_target_pairs={{1,0},{2,1},{3,2},{4,3},{5,4},{6,5},{7,6},{8,7},{9,8},{10,9},{11,1... | collective-permute-start | bytes 368648 | tf_op jit(solution)/shard_map/ppermute | solution.py:34
  545.0 15.5 %collective-permute-start.6 = (bf16[5,1,8,8,192]{4,3,2,1,0:T(8,128)(2,1)S(1)}, bf16[5,1,8,8,192]{4,3,2,1,0:T(8,128)(2,1)S(1)}, u32[]{:S(2)}, u32[]{:S(2)}) collective-permute-start(bf16[5,1,8,8,192]{4,3,2,1,0:T(8,128)(2,1)S(1)} %get-tuple-element.14), channel_id=1, source_target_pairs={{0,1},{1,2},{2,3},{3,4},{4,5},{5,6},{6,7},{7,8},{8,9},{9,10},{10,1... | collective-permute-start | bytes 368648 | tf_op jit(solution)/shard_map/ppermute | solution.py:33
  644.6 543.1 %copy-start.5 = (f32[8,13,192]{2,1,0:T(8,128)S(1)}, f32[8,13,192]{2,1,0:T(8,128)}, u32[]{:S(2)}) copy-start(f32[8,13,192]{2,1,0:T(8,128)} %copy-done.4) | copy-start | bytes 239620
  1094.4 117.7 %copy-start.12 = (f32[8,192]{1,0:T(8,128)S(1)}, f32[8,192]{1,0:T(8,128)}, u32[]{:S(2)}) copy-start(f32[8,192]{1,0:T(8,128)} %reduce_sum.83) | copy-start | bytes 18436
  1169.5 5.3 collective-permute-start.9
  1170.8 5.0 collective-permute-start.8
  1175.8 9.9 collective-permute-start.11
  1179.5 7.5 collective-permute-start.10
  1193.6 5.5 collective-permute-start.13
  1194.9 5.8 collective-permute-start.12
  1200.8 16.8 %collective-permute-start.15 = (bf16[5,1,8,8,192]{4,3,2,1,0:T(8,128)(2,1)S(1)}, bf16[5,1,8,8,192]{4,3,2,1,0:T(8,128)(2,1)S(1)}, u32[]{:S(2)}, u32[]{:S(2)}) collective-permute-start(bf16[5,1,8,8,192]{4,3,2,1,0:T(8,128)(2,1)S(1)} %get-tuple-element.13), channel_id=1, source_target_pairs={{1,0},{2,1},{3,2},{4,3},{5,4},{6,5},{7,6},{8,7},{9,8},{10,9},{11,1... | collective-permute-start | bytes 368648 | tf_op jit(solution)/shard_map/ppermute | solution.py:34
  1202.7 14.9 %collective-permute-start.14 = (bf16[5,1,8,8,192]{4,3,2,1,0:T(8,128)(2,1)S(1)}, bf16[5,1,8,8,192]{4,3,2,1,0:T(8,128)(2,1)S(1)}, u32[]{:S(2)}, u32[]{:S(2)}) collective-permute-start(bf16[5,1,8,8,192]{4,3,2,1,0:T(8,128)(2,1)S(1)} %get-tuple-element.12), channel_id=1, source_target_pairs={{0,1},{1,2},{2,3},{3,4},{4,5},{5,6},{6,7},{7,8},{8,9},{9,10},{10,1... | collective-permute-start | bytes 368648 | tf_op jit(solution)/shard_map/ppermute | solution.py:33
Sparse Core Ops, SparseCore 0:
  9.9 447.8 all-gather.4
  643.4 438.5 all-gather.6
